TPU v7x, 32 devices: a whole 2x2x4 slice. The times are simulated.
32 devices in a mesh: row: 8 (over y, x, core), col: 4 (over z).
Axes of the slice: x: 2, y: 2, z: 4, core: 2. Of those that a mesh axis runs over, the one named last changes fastest.
Arguments:
- features: bfloat16 [6144, 256], P(('col', 'row')), may hold values from -6 to 6
- edge_tiles: bfloat16 [8, 4, 12, 256, 256], P('row', 'col'), may hold values from 0.006225586 to 0.0625
- tile_rows: int32 [8, 4, 12], P('row', 'col'), may hold values from 0 to 2, as said below
- tile_cols: int32 [8, 4, 12], P('row', 'col'), may hold values from 0 to 5
- tile_count: int32 [8, 4], P('row', 'col'), may hold values from 3 to 12, as said below
- weight: bfloat16 [256, 256], replicated, may hold values from -0.375 to 0.375
- cotangent: bfloat16 [6144, 256], P(('row', 'col')), may hold values from -6 to 6
Outputs:
- activated: bfloat16 [6144, 256], P(('row', 'col'))
- feature_grad: bfloat16 [6144, 256], P(('col', 'row'))
Inputs may be any that keep to these rules, and one draw needn't show every extreme that they name: Within one device the pairs (tile_rows, tile_cols) of all 12 slots are distinct. Slots at or past tile_count hold no edges of the graph.
All inputs are finite; a program needn't handle non-finite values.
Results may differ from a plain program's by a relative error of at most 0.006.
Values may be sent and summed in bfloat16 or wider, within the bound.
No kernel may reach another device: no remote copies, remote signals or barrier semaphores. Data moves between devices by JAX's collectives and lax.ppermute only.
A program may use at most 64 MiB of HBM per device.

v0:
```python
import jax
import jax.numpy as jnp
from jax import lax
from jax.sharding import PartitionSpec as P


def silu_slope(mixed):
    sigma = jax.nn.sigmoid(mixed)
    return sigma * (1.0 + mixed * (1.0 - sigma))


def dense_layer(summed, grad_rows, weight):
    aggregated = summed.astype(jnp.bfloat16)
    mixed = jnp.dot(aggregated, weight, preferred_element_type=jnp.float32)
    activated = jax.nn.silu(mixed).astype(jnp.bfloat16)
    scaled = (grad_rows.astype(jnp.float32) * silu_slope(mixed)).astype(jnp.bfloat16)
    pulled = jnp.dot(scaled, weight.T, preferred_element_type=jnp.float32).astype(jnp.bfloat16)
    return (activated, pulled)


def place(results, targets, occupied, count):
    masked = results * occupied[:, None, None]
    return jax.ops.segment_sum(masked, targets, num_segments=count)


def on_device(features, edge_tiles, tile_rows, tile_cols, tile_count, weight, cotangent):
    blocks = edge_tiles[0, 0]
    row_slots = tile_rows[0, 0]
    col_slots = tile_cols[0, 0]
    filled = tile_count[0, 0]
    slot_total = blocks.shape[0]
    tile_size = blocks.shape[1]
    feat_width = features.shape[1]
    own_rows = features.shape[0]
    row_tiles = own_rows * lax.axis_size("col") // tile_size
    col_tiles = own_rows * lax.axis_size("row") // tile_size
    occupied = (jnp.arange(slot_total, dtype=jnp.int32) < filled).astype(jnp.float32)
    gathered = lax.all_gather(features, "row", axis=0, tiled=True)
    picked = gathered.reshape(col_tiles, tile_size, feat_width)[col_slots]
    products = jnp.einsum("kij,kjf->kif", blocks, picked, preferred_element_type=jnp.float32)
    partial_value = place(products, row_slots, occupied, row_tiles).reshape(
        row_tiles * tile_size, feat_width
    )
    own_sums = lax.psum_scatter(partial_value, "col", scatter_dimension=0, tiled=True)
    activated, pulled_own = dense_layer(own_sums, cotangent, weight)
    pulled_block = lax.all_gather(pulled_own, "col", axis=0, tiled=True)
    chosen = pulled_block.reshape(row_tiles, tile_size, feat_width)[row_slots]
    flipped = jnp.einsum("kij,kif->kjf", blocks, chosen, preferred_element_type=jnp.float32)
    partial_grad = place(flipped, col_slots, occupied, col_tiles).reshape(
        col_tiles * tile_size, feat_width
    )
    feature_grad = lax.psum_scatter(partial_grad, "row", scatter_dimension=0, tiled=True).astype(
        jnp.bfloat16
    )
    return (activated, feature_grad)


def solution(mesh):
    return jax.shard_map(
        on_device,
        mesh=mesh,
        in_specs=(
            P(("col", "row"), None),
            P("row", "col", None, None, None),
            P("row", "col", None),
            P("row", "col", None),
            P("row", "col"),
            P(),
            P(("row", "col"), None),
        ),
        out_specs=(P(("row", "col"), None), P(("col", "row"), None)),
        check_vma=False,
    )
```

profile of v0, /device:TPU:0, one launch (start us, length us, event | category | flops | bytes accessed | tf_op | source)
XLA Modules:
  0.0 138.2 jit_solution(2664074008607419204)
XLA Ops:
  7.2 0.0 copy-start
  7.2 0.0 reduce-scatter.3.cloned.1.call-start
  8.0 12.2 %all_gather.6 = bf16[1536,256]{1,0:T(8,128)(2,1)S(1)} all-gather(bf16[192,256]{1,0:T(8,128)(2,1)} %param.7), channel_id=1, replica_groups=mesh['row'=8,'col'=4] {'row'}, dimensions={0}, use_global_device_ids=true | all-gather | bytes 884736 | tf_op jit(solution)/shard_map/all_gather | solution.py:38
  20.2 0.7 fusion.4
  20.9 1.8 %gather_fusion = bf16[12,256,256]{2,1,0:T(8,128)(2,1)} fusion(bf16[6,256,256]{2,1,0:T(8,128)(2,1)S(1)} %bitcast.32, s32[1024]{0:T(1024)S(1)} %pad_clamp_fusion.1), kind=kCustom, calls=%fused_computation | custom fusion | bytes 3145776 | tf_op jit(solution)/shard_map/gather | solution.py:39
  22.7 0.0 copy-done
  22.7 3.8 %multiply_bitcast_fusion.1 = f32[12,256,256]{1,2,0:T(8,128)} fusion(bf16[12,256,256]{2,1,0:T(8,128)(2,1)} %gather_fusion, bf16[1,1,12,256,256]{4,3,2,1,0:T(8,128)(2,1)S(1)} %copy-done, f32[12]{0:T(128)S(1)} %compare_convert_fusion), kind=kOutput, calls=%fused_computation.5 | convolution fusion | flops 403439616 | bytes 6291504 | tf_op jit(solution)/shard_map/kij,kjf->kif/dot_general | solution.py:40
  26.6 3.6 %copy.12 = f32[12,256,256]{2,1,0:T(8,128)} copy(f32[12,256,256]{1,2,0:T(8,128)} %multiply_bitcast_fusion.1) | data formatting | bytes 6291456 | tf_op jit(solution)/shard_map/mul | solution.py:22
  30.1 0.1 broadcast_in_dim.4
  30.2 0.0 copy-done.3
  30.2 0.0 copy-start.5
  30.2 5.7 %scatter_fusion = f32[3,256,256]{2,1,0:T(8,128)S(1)} fusion(f32[3,256,256]{2,1,0:T(8,128)S(1)} %broadcast_in_dim.4, s32[12]{0:T(128)S(1)} %bitcast.33, f32[12,256,256]{2,1,0:T(8,128)} %copy.12), kind=kCustom, calls=%fused_computation.2 | custom fusion | flops 786432 | bytes 9437232 | tf_op jit(solution)/shard_map/scatter-add | solution.py:23
  36.0 0.0 copy-start.1
  36.0 0.0 copy-start.6
  36.0 0.9 copy-done.1
  36.8 0.0 reduce-scatter.3.cloned.1.call-update
  36.9 0.0 reduce-scatter.5.cloned.1.call-start
  36.9 23.5 %reduce-scatter.3.cloned.1.call-done = f32[192,256]{1,0:T(8,128)} async-done(((f32[768,256]{1,0:T(8,128)}), f32[192,256]{1,0:T(8,128)}) %reduce-scatter.3.cloned.1.call-update) | async-done | bytes 196624 | tf_op jit(solution)/shard_map/reduce_scatter | solution.py:44
  60.5 0.0 copy-done.5
  60.5 1.8 %multiply_convert_fusion.1 = (bf16[192,256]{1,0:T(8,128)(2,1)}, f32[192,256]{1,0:T(8,128)S(1)}) fusion(bf16[256,256]{1,0:T(8,128)(2,1)S(1)} %copy-done.5, f32[192,256]{1,0:T(8,128)} %reduce-scatter.3.cloned.1.call-done), kind=kOutput, calls=%fused_computation.10 | convolution fusion | flops 25460736 | bytes 622592 | tf_op jit(solution)/shard_map/dot_general | solution.py:14
  62.3 0.2 convolution_convert_fusion
  62.5 15.2 %all_gather.7 = bf16[768,256]{1,0:T(8,128)(2,1)S(1)} all-gather(bf16[192,256]{1,0:T(8,128)(2,1)S(1)} %convolution_convert_fusion), channel_id=1, replica_groups=mesh['row'=8,'col'=4] {'col'}, dimensions={0}, use_global_device_ids=true | all-gather | bytes 491520 | tf_op jit(solution)/shard_map/all_gather | solution.py:46
  77.7 0.6 gather_fusion.1
  78.4 2.4 %multiply_bitcast_fusion = f32[12,256,256]{1,2,0:T(8,128)} fusion(bf16[12,256,256]{2,1,0:T(8,128)(2,1)S(1)} %gather_fusion.1, bf16[1,1,12,256,256]{4,3,2,1,0:T(8,128)(2,1)S(1)} %copy-done, f32[12]{0:T(128)S(1)} %compare_convert_fusion), kind=kOutput, calls=%fused_computation.4 | convolution fusion | flops 403439616 | bytes 6291504 | tf_op jit(solution)/shard_map/kij,kif->kjf/dot_general | solution.py:48
  80.8 3.6 %copy.14 = f32[12,256,256]{2,1,0:T(8,128)} copy(f32[12,256,256]{1,2,0:T(8,128)} %multiply_bitcast_fusion) | data formatting | bytes 6291456 | tf_op jit(solution)/shard_map/mul | solution.py:22
  84.4 0.1 broadcast_in_dim.5
  84.5 0.5 copy-done.4
  85.0 5.8 %scatter_fusion.1 = f32[6,256,256]{2,1,0:T(8,128)S(1)} fusion(f32[6,256,256]{2,1,0:T(8,128)S(1)} %broadcast_in_dim.5, s32[12]{0:T(128)S(1)} %bitcast.34, f32[12,256,256]{2,1,0:T(8,128)} %copy.14), kind=kCustom, calls=%fused_computation.3 | custom fusion | flops 786432 | bytes 9437232 | tf_op jit(solution)/shard_map/scatter-add | solution.py:23
  90.8 1.2 copy-done.2
  91.9 0.0 reduce-scatter.5.cloned.1.call-update
  92.0 37.8 %reduce-scatter.5.cloned.1.call-done = f32[192,256]{1,0:T(8,128)} async-done(((f32[1536,256]{1,0:T(8,128)}), f32[192,256]{1,0:T(8,128)}) %reduce-scatter.5.cloned.1.call-update) | async-done | bytes 196624 | tf_op jit(solution)/shard_map/reduce_scatter | solution.py:52
  129.8 1.6 %convert_element_type.31 = bf16[192,256]{1,0:T(8,128)(2,1)} convert(f32[192,256]{1,0:T(8,128)} %reduce-scatter.5.cloned.1.call-done) | non-fusion elementwise | flops 49152 | bytes 294912 | tf_op jit(solution)/shard_map/convert_element_type | solution.py:52
  (8 shorter events, 0.0 us)
Async XLA Ops:
  7.2 15.6 %copy-start = (bf16[1,1,12,256,256]{4,3,2,1,0:T(8,128)(2,1)S(1)}, bf16[1,1,12,256,256]{4,3,2,1,0:T(8,128)(2,1)}, u32[]{:S(2)}) copy-start(bf16[1,1,12,256,256]{4,3,2,1,0:T(8,128)(2,1)} %param.8) | copy-start | bytes 4718596
  7.2 53.3 %reduce-scatter.3.cloned.1.call-start = ((), (), s32[]{:S(2)}) async-start(), calls=%async_computation.2 | async-start | bytes 983040 | tf_op jit(solution)/shard_map/reduce_scatter | solution.py:44
  26.6 3.6 %copy-start.3 = (s32[1,1,12]{2,1,0:T(1,128)S(1)}, s32[1,1,12]{2,1,0:T(1,128)}, u32[]{:S(2)}) copy-start(s32[1,1,12]{2,1,0:T(1,128)} %param.9) | copy-start | bytes 148
  30.2 30.3 %copy-start.5 = (bf16[256,256]{1,0:T(8,128)(2,1)S(1)}, bf16[256,256]{1,0:T(8,128)(2,1)}, u32[]{:S(2)}) copy-start(bf16[256,256]{1,0:T(8,128)(2,1)} %param.12) | copy-start | bytes 393220
  36.0 0.9 copy-start.1
  36.0 26.3 %copy-start.6 = (bf16[192,256]{1,0:T(8,128)(2,1)S(1)}, bf16[192,256]{1,0:T(8,128)(2,1)}, u32[]{:S(2)}) copy-start(bf16[192,256]{1,0:T(8,128)(2,1)} %param.13) | copy-start | bytes 294916
  36.9 92.9 %reduce-scatter.5.cloned.1.call-start = ((), (), s32[]{:S(2)}) async-start(), calls=%async_computation.3 | async-start | bytes 1769472 | tf_op jit(solution)/shard_map/reduce_scatter | solution.py:52
  84.3 0.7 copy-start.4
  90.8 1.2 copy-start.2
Sparse Core Ops, SparseCore 0:
  37.0 23.4 reduce-scatter.2
  92.1 37.6 reduce-scatter.4
where the time goes:
time: 139 us; the launch traced here: 138 us
  waiting for transfers between devices  61.4 us (44%)
  blocking collectives  27.5 us (20%)
  between operations  14.9 us (11%)
  other arithmetic  13.7 us (10%)
  local copies, waits for them, and re-layouts  12.4 us (9%)
  matrix products  8.22 us (6%)
    reduce_scatter x1, waiting for transfers between devices, on_device(): lax.psum_scatter(partial_grad, 'row', scatter_dimension=0, tiled=True)  37.8 us
    reduce_scatter x1, waiting for transfers between devices, on_device(): lax.psum_scatter(partial_value, 'col', scatter_dimension=0, tiled=True)  23.5 us
    all_gather x1, blocking collectives, on_device(): pulled_block = lax.all_gather(pulled_own, 'col', axis=0, tiled=True)  15.2 us
    all_gather x1, blocking collectives, on_device(): gathered = lax.all_gather(features, 'row', axis=0, tiled=True)  12.2 us
    scatter-add x2, other arithmetic, place(): return jax.ops.segment_sum(masked, targets, num_segments=count)  11.5 us
    mul x2, local copies, waits for them, and re-layouts, place(): masked = results * occupied[:, None, None]  7.13 us
    dot_general x1, matrix products, on_device(): jnp.einsum('kij,kjf->kif', blocks, picked, preferred_element_type=jnp.flo...  3.81 us
  transfers between devices with their start and end apart: 2, of which 2 were waited for; matrix products, arithmetic and copies ran while one was open for 0% of the time, Pallas kernels for 0%

commit v1 on v0

--- a/solution.py
+++ b/solution.py
@@ -43,7 +43,18 @@
     )
     own_sums = lax.psum_scatter(partial_value, "col", scatter_dimension=0, tiled=True)
     activated, pulled_own = dense_layer(own_sums, cotangent, weight)
-    pulled_block = lax.all_gather(pulled_own, "col", axis=0, tiled=True)
+    n_all = lax.axis_size("col")
+    panels = tuple(((hop_no, (hop_no + 1) % n_all) for hop_no in range(n_all)))
+    pieces_in = tuple(((hop_no, (hop_no - 1) % n_all) for hop_no in range(n_all)))
+    local_out, value_now = ([pulled_own], [pulled_own])
+    for _ in range(n_all // 2):
+        local_out.append(lax.ppermute(local_out[-1], perm=panels, axis_name="col"))
+    for _ in range((n_all - 1) // 2):
+        value_now.append(lax.ppermute(value_now[-1], axis_name="col", perm=pieces_in))
+    after = jnp.concatenate([*local_out[::-1], *value_now[1:]], axis=0)
+    pulled_block = jnp.roll(
+        after, (lax.axis_index("col") - n_all // 2) * pulled_own.shape[0], axis=0
+    )
     chosen = pulled_block.reshape(row_tiles, tile_size, feat_width)[row_slots]
     flipped = jnp.einsum("kij,kif->kjf", blocks, chosen, preferred_element_type=jnp.float32)
     partial_grad = place(flipped, col_slots, occupied, col_tiles).reshape(

time: 139 us -> 139 us (level)
  blocking collectives: 27.5 us -> 12.2 us
  waiting for transfers between devices: 61.4 us -> 72.4 us
  starting transfers between devices: 0.08 us -> 3.96 us
    all_gather x1 -> x0, blocking collectives: 15.2 us -> none  [on_device(): pulled_block = lax.all_gather(pulled_own, 'col', axis=0, tiled=True)]
    ppermute x0 -> x3, waiting for transfers between devices: none -> 8.98 us  [the longest x2 8.98 us: on_device(): local_out.append(lax.ppermute(local_out[-1], perm=panels, axis_name='col'))]
    ppermute x0 -> x3, starting transfers between devices: none -> 3.88 us  [the longest x1 3.82 us: on_device(): lax.ppermute(value_now[-1], axis_name='col', perm=pieces_in)]
    reduce_scatter x1, waiting for transfers between devices: 37.8 us -> 39.8 us  [on_device(): lax.psum_scatter(partial_grad, 'row', scatter_dimension=0, tiled=True)]
  transfers between devices with their start and end apart: 2 -> 5, of which waited for: 2 -> 4; matrix products, arithmetic and copies ran while one was open for 0% -> 0% of each run, Pallas kernels for 0% -> 0%
where the time goes in v1:
time: 139 us; the launch traced here: 138 us
  waiting for transfers between devices  72.4 us (52%)
  between operations  15 us (11%)
  other arithmetic  13.7 us (10%)
  local copies, waits for them, and re-layouts  12.5 us (9%)
  blocking collectives  12.2 us (9%)
  matrix products  8.24 us (6%)
  starting transfers between devices  3.96 us (3%)
    reduce_scatter x1, waiting for transfers between devices, on_device(): lax.psum_scatter(partial_grad, 'row', scatter_dimension=0, tiled=True)  39.8 us
    reduce_scatter x1, waiting for transfers between devices, on_device(): lax.psum_scatter(partial_value, 'col', scatter_dimension=0, tiled=True)  23.5 us
    all_gather x1, blocking collectives, on_device(): gathered = lax.all_gather(features, 'row', axis=0, tiled=True)  12.2 us
    scatter-add x2, other arithmetic, place(): return jax.ops.segment_sum(masked, targets, num_segments=count)  11.5 us
    ppermute x2, waiting for transfers between devices, on_device(): local_out.append(lax.ppermute(local_out[-1], perm=panels, axis_name='col'))  8.98 us
    mul x2, local copies, waits for them, and re-layouts, place(): masked = results * occupied[:, None, None]  7.11 us
    ppermute x1, starting transfers between devices, on_device(): lax.ppermute(value_now[-1], axis_name='col', perm=pieces_in)  3.82 us
    dot_general x1, matrix products, on_device(): jnp.einsum('kij,kjf->kif', blocks, picked, preferred_element_type=jnp.flo...  3.81 us
  transfers between devices with their start and end apart: 5, of which 4 were waited for; matrix products, arithmetic and copies ran while one was open for 0% of the time, Pallas kernels for 0%

profile of v1, /device:TPU:0, one launch (start us, length us, event | category | flops | bytes accessed | tf_op | source)
XLA Modules:
  0.0 138.1 jit_solution(15030874265350349775)
XLA Ops:
  7.2 0.0 copy-start
  7.2 0.0 reduce-scatter.3.cloned.1.call-start
  8.0 12.2 %all_gather.3 = bf16[1536,256]{1,0:T(8,128)(2,1)S(1)} all-gather(bf16[192,256]{1,0:T(8,128)(2,1)} %param.7), channel_id=1, replica_groups=mesh['row'=8,'col'=4] {'row'}, dimensions={0}, use_global_device_ids=true | all-gather | bytes 884736 | tf_op jit(solution)/shard_map/all_gather | solution.py:38
  20.2 0.7 fusion.4
  20.9 1.9 %gather_fusion = bf16[12,256,256]{2,1,0:T(8,128)(2,1)} fusion(bf16[6,256,256]{2,1,0:T(8,128)(2,1)S(1)} %bitcast.32, s32[1024]{0:T(1024)S(1)} %pad_clamp_fusion.1), kind=kCustom, calls=%fused_computation | custom fusion | bytes 3145776 | tf_op jit(solution)/shard_map/gather | solution.py:39
  22.8 3.8 %multiply_bitcast_fusion.1 = f32[12,256,256]{1,2,0:T(8,128)} fusion(bf16[12,256,256]{2,1,0:T(8,128)(2,1)} %gather_fusion, bf16[1,1,12,256,256]{4,3,2,1,0:T(8,128)(2,1)S(1)} %copy-done, f32[12]{0:T(128)S(1)} %compare_convert_fusion), kind=kOutput, calls=%fused_computation.5 | convolution fusion | flops 403439616 | bytes 6291504 | tf_op jit(solution)/shard_map/kij,kjf->kif/dot_general | solution.py:40
  26.6 3.6 %copy.12 = f32[12,256,256]{2,1,0:T(8,128)} copy(f32[12,256,256]{1,2,0:T(8,128)} %multiply_bitcast_fusion.1) | data formatting | bytes 6291456 | tf_op jit(solution)/shard_map/mul | solution.py:22
  30.1 0.1 broadcast_in_dim.4
  30.2 0.0 copy-start.5
  30.2 5.7 %scatter_fusion = f32[3,256,256]{2,1,0:T(8,128)S(1)} fusion(f32[3,256,256]{2,1,0:T(8,128)S(1)} %broadcast_in_dim.4, s32[12]{0:T(128)S(1)} %bitcast.33, f32[12,256,256]{2,1,0:T(8,128)} %copy.12), kind=kCustom, calls=%fused_computation.2 | custom fusion | flops 786432 | bytes 9437232 | tf_op jit(solution)/shard_map/scatter-add | solution.py:23
  36.0 0.0 copy-start.6
  36.0 0.9 copy-done.1
  36.9 0.0 reduce-scatter.3.cloned.1.call-update
  36.9 0.0 reduce-scatter.5.cloned.1.call-start
  36.9 23.5 %reduce-scatter.3.cloned.1.call-done = f32[192,256]{1,0:T(8,128)} async-done(((f32[768,256]{1,0:T(8,128)}), f32[192,256]{1,0:T(8,128)}) %reduce-scatter.3.cloned.1.call-update) | async-done | bytes 196624 | tf_op jit(solution)/shard_map/reduce_scatter | solution.py:44
  60.5 1.8 %multiply_convert_fusion.1 = (bf16[192,256]{1,0:T(8,128)(2,1)}, f32[192,256]{1,0:T(8,128)S(1)}) fusion(bf16[256,256]{1,0:T(8,128)(2,1)S(1)} %copy-done.5, f32[192,256]{1,0:T(8,128)} %reduce-scatter.3.cloned.1.call-done), kind=kOutput, calls=%fused_computation.10 | convolution fusion | flops 25460736 | bytes 622592 | tf_op jit(solution)/shard_map/dot_general | solution.py:14
  62.3 0.2 convolution_convert_fusion
  62.5 0.1 collective-permute-start
  62.6 6.4 %collective-permute-done = bf16[192,256]{1,0:T(8,128)(2,1)S(1)} collective-permute-done((bf16[192,256]{1,0:T(8,128)(2,1)S(1)}, bf16[192,256]{1,0:T(8,128)(2,1)S(1)}, u32[]{:S(2)}, u32[]{:S(2)}) %collective-permute-start) | collective-permute-done | bytes 98336 | tf_op jit(solution)/shard_map/ppermute | solution.py:51
  69.0 3.8 %collective-permute-start.2 = (bf16[192,256]{1,0:T(8,128)(2,1)S(1)}, bf16[192,256]{1,0:T(8,128)(2,1)S(1)}, u32[]{:S(2)}, u32[]{:S(2)}) collective-permute-start(bf16[192,256]{1,0:T(8,128)(2,1)S(1)} %convolution_convert_fusion), channel_id=1, source_target_pairs={{0,3},{1,0},{2,1},{3,2},{4,7},{5,4},{6,5},{7,6},{8,11},{9,8},{10,9... | collective-permute-start | bytes 294920 | tf_op jit(solution)/shard_map/ppermute | solution.py:53
  72.8 2.6 %collective-permute-done.1 = bf16[192,256]{1,0:T(8,128)(2,1)S(1)} collective-permute-done((bf16[192,256]{1,0:T(8,128)(2,1)S(1)}, bf16[192,256]{1,0:T(8,128)(2,1)S(1)}, u32[]{:S(2)}, u32[]{:S(2)}) %collective-permute-start.1) | collective-permute-done | bytes 98336 | tf_op jit(solution)/shard_map/ppermute | solution.py:51
  75.5 0.1 constant_dynamic-slice_fusion
  75.7 0.6 gather_fusion.1
  76.3 2.4 %multiply_bitcast_fusion = f32[12,256,256]{1,2,0:T(8,128)} fusion(bf16[12,256,256]{2,1,0:T(8,128)(2,1)S(1)} %gather_fusion.1, bf16[1,1,12,256,256]{4,3,2,1,0:T(8,128)(2,1)S(1)} %copy-done, f32[12]{0:T(128)S(1)} %compare_convert_fusion), kind=kOutput, calls=%fused_computation.4 | convolution fusion | flops 403439616 | bytes 6291504 | tf_op jit(solution)/shard_map/kij,kif->kjf/dot_general | solution.py:59
  78.7 3.6 %copy.14 = f32[12,256,256]{2,1,0:T(8,128)} copy(f32[12,256,256]{1,2,0:T(8,128)} %multiply_bitcast_fusion) | data formatting | bytes 6291456 | tf_op jit(solution)/shard_map/mul | solution.py:22
  82.3 0.1 broadcast_in_dim.5
  82.4 0.5 copy-done.4
  82.9 5.8 %scatter_fusion.1 = f32[6,256,256]{2,1,0:T(8,128)S(1)} fusion(f32[6,256,256]{2,1,0:T(8,128)S(1)} %broadcast_in_dim.5, s32[12]{0:T(128)S(1)} %bitcast.34, f32[12,256,256]{2,1,0:T(8,128)} %copy.14), kind=kCustom, calls=%fused_computation.3 | custom fusion | flops 786432 | bytes 9437232 | tf_op jit(solution)/shard_map/scatter-add | solution.py:23
  88.7 1.1 copy-done.2
  89.8 0.0 reduce-scatter.5.cloned.1.call-update
  89.9 39.8 %reduce-scatter.5.cloned.1.call-done = f32[192,256]{1,0:T(8,128)} async-done(((f32[1536,256]{1,0:T(8,128)}), f32[192,256]{1,0:T(8,128)}) %reduce-scatter.5.cloned.1.call-update) | async-done | bytes 196624 | tf_op jit(solution)/shard_map/reduce_scatter | solution.py:63
  129.7 1.6 %convert_element_type.31 = bf16[192,256]{1,0:T(8,128)(2,1)} convert(f32[192,256]{1,0:T(8,128)} %reduce-scatter.5.cloned.1.call-done) | non-fusion elementwise | flops 49152 | bytes 294912 | tf_op jit(solution)/shard_map/convert_element_type | solution.py:63
  (22 shorter events, 0.1 us)
Async XLA Ops:
  7.2 15.6 %copy-start = (bf16[1,1,12,256,256]{4,3,2,1,0:T(8,128)(2,1)S(1)}, bf16[1,1,12,256,256]{4,3,2,1,0:T(8,128)(2,1)}, u32[]{:S(2)}) copy-start(bf16[1,1,12,256,256]{4,3,2,1,0:T(8,128)(2,1)} %param.8) | copy-start | bytes 4718596
  7.2 53.3 %reduce-scatter.3.cloned.1.call-start = ((), (), s32[]{:S(2)}) async-start(), calls=%async_computation.2 | async-start | bytes 983040 | tf_op jit(solution)/shard_map/reduce_scatter | solution.py:44
  26.6 3.6 %copy-start.3 = (s32[1,1,12]{2,1,0:T(1,128)S(1)}, s32[1,1,12]{2,1,0:T(1,128)}, u32[]{:S(2)}) copy-start(s32[1,1,12]{2,1,0:T(1,128)} %param.9) | copy-start | bytes 148
  30.2 30.3 %copy-start.5 = (bf16[256,256]{1,0:T(8,128)(2,1)S(1)}, bf16[256,256]{1,0:T(8,128)(2,1)}, u32[]{:S(2)}) copy-start(bf16[256,256]{1,0:T(8,128)(2,1)} %param.12) | copy-start | bytes 393220
  36.0 0.9 copy-start.1
  36.0 26.3 %copy-start.6 = (bf16[192,256]{1,0:T(8,128)(2,1)S(1)}, bf16[192,256]{1,0:T(8,128)(2,1)}, u32[]{:S(2)}) copy-start(bf16[192,256]{1,0:T(8,128)(2,1)} %param.13) | copy-start | bytes 294916
  36.9 92.8 %reduce-scatter.5.cloned.1.call-start = ((), (), s32[]{:S(2)}) async-start(), calls=%async_computation.3 | async-start | bytes 1769472 | tf_op jit(solution)/shard_map/reduce_scatter | solution.py:63
  62.5 6.5 %collective-permute-start = (bf16[192,256]{1,0:T(8,128)(2,1)S(1)}, bf16[192,256]{1,0:T(8,128)(2,1)S(1)}, u32[]{:S(2)}, u32[]{:S(2)}) collective-permute-start(bf16[192,256]{1,0:T(8,128)(2,1)S(1)} %convolution_convert_fusion), channel_id=1, source_target_pairs={{0,1},{1,2},{2,3},{3,0},{4,5},{5,6},{6,7},{7,4},{8,9},{9,10},{10,1... | collective-permute-start | bytes 294920 | tf_op jit(solution)/shard_map/ppermute | solution.py:51
  69.0 6.4 %collective-permute-start.1 = (bf16[192,256]{1,0:T(8,128)(2,1)S(1)}, bf16[192,256]{1,0:T(8,128)(2,1)S(1)}, u32[]{:S(2)}, u32[]{:S(2)}) collective-permute-start(bf16[192,256]{1,0:T(8,128)(2,1)S(1)} %collective-permute-done), channel_id=1, source_target_pairs={{0,1},{1,2},{2,3},{3,0},{4,5},{5,6},{6,7},{7,4},{8,9},{9,10},{10,1... | collective-permute-start | bytes 294920 | tf_op jit(solution)/shard_map/ppermute | solution.py:51
  69.0 6.5 %collective-permute-start.2 = (bf16[192,256]{1,0:T(8,128)(2,1)S(1)}, bf16[192,256]{1,0:T(8,128)(2,1)S(1)}, u32[]{:S(2)}, u32[]{:S(2)}) collective-permute-start(bf16[192,256]{1,0:T(8,128)(2,1)S(1)} %convolution_convert_fusion), channel_id=1, source_target_pairs={{0,3},{1,0},{2,1},{3,2},{4,7},{5,4},{6,5},{7,6},{8,11},{9,8},{10,9... | collective-permute-start | bytes 294920 | tf_op jit(solution)/shard_map/ppermute | solution.py:53
  82.3 0.7 copy-start.4
  88.7 1.2 copy-start.2
Sparse Core Ops, SparseCore 0:
  37.0 23.4 reduce-scatter.2
  90.0 39.6 reduce-scatter.4
